TPU v7x, 256 devices: a whole 4x4x8 slice. The times are simulated.
256 devices in a mesh: dp: 16 (over x, y_hi, core), seq: 16 (over z, y_lo).
Axes of the slice: x: 4, y: 4 (y_hi: 2, y_lo: 2; y = y_hi * 2 + y_lo), z: 8, core: 2. Of those that a mesh axis runs over, the one named last changes fastest.
Arguments:
- queries: bfloat16 [40960, 768], P(('dp', 'seq')), may hold values from -8 to 8
- keys: bfloat16 [40960, 768], P(('dp', 'seq')), may hold values from -8 to 8
- values: bfloat16 [40960, 768], P(('dp', 'seq')), may hold values from -6 to 6
- frames: bfloat16 [40960, 768], P(('dp', 'seq')), may hold values from -4 to 4
- upstream: bfloat16 [40960, 768], P(('dp', 'seq')), may hold values from -6 to 6
- lengths: int32 [16], P('dp'), may hold values from 640 to 2560, as said below
- conv_kernel: bfloat16 [32, 768], replicated, may hold values from -1 to 1
Outputs:
- out: bfloat16 [40960, 768], P(('dp', 'seq'))
- query_grad: bfloat16 [40960, 768], P(('dp', 'seq'))
- key_grad: bfloat16 [40960, 768], P(('dp', 'seq'))
- value_grad: bfloat16 [40960, 768], P(('dp', 'seq'))
- frame_grad: bfloat16 [40960, 768], P(('dp', 'seq'))
- kernel_grad: float32 [32, 768], replicated
Inputs may be any that keep to these rules, and one draw needn't show every extreme that they name: `lengths`: one utterance has all 2560 frames live and another has 640.
All inputs are finite; a program needn't handle non-finite values.
Results may differ from a plain program's by a relative error of at most 0.0262.
Values may be sent and summed in bfloat16 or wider, within the bound.
No kernel may reach another device: no remote copies, remote signals or barrier semaphores. Data moves between devices by JAX's collectives and lax.ppermute only.
A program may use at most 128 MiB of HBM per device.

v0:
```python
import jax
import jax.numpy as jnp
from jax import lax
from jax.sharding import PartitionSpec as P

HEAD_DIM = 64
KERNEL = 32


def shifted(x, axis, by):
    count = lax.axis_size(axis)
    pairs = [(i, i + by) for i in range(count) if 0 <= i + by < count]
    return lax.ppermute(x, axis, pairs)


def per_device(queries, keys, values, frames, upstream, lengths, conv_kernel):
    row_count = queries.shape[0]
    channels = queries.shape[1]
    head_count = channels // HEAD_DIM
    seq_count = lax.axis_size("seq")
    first_row = lax.axis_index("seq") * row_count
    length = lengths[0]
    score_scale = HEAD_DIM ** (-0.5)
    span = row_count * seq_count
    shards = 1
    while shards * row_count < 512 and seq_count % (2 * shards) == 0:
        shards = shards * 2
    key_block = row_count * shards
    block_count = span // key_block
    key_all, value_all = (
        lax.all_gather(keys, "seq", axis=0, tiled=True),
        lax.all_gather(values, "seq", axis=0, tiled=True),
    )
    key_blocks = key_all.reshape(block_count, key_block, head_count, HEAD_DIM)
    value_blocks = value_all.reshape(block_count, key_block, head_count, HEAD_DIM)
    block_starts = jnp.arange(block_count, dtype=jnp.int32) * key_block
    query_heads = queries.reshape(row_count, head_count, HEAD_DIM)

    def block_scores(key_part, block_start):
        scores = (
            jnp.einsum("thd,khd->htk", query_heads, key_part, preferred_element_type=jnp.float32)
            * score_scale
        )
        key_live = block_start + jnp.arange(key_part.shape[0], dtype=jnp.int32) < length
        return jnp.where(key_live[None, None, :], scores, -jnp.inf)

    def running_total(state_pair, block_items):
        running_top, total_sum = state_pair
        key_part, block_start = block_items
        scores = block_scores(key_part, block_start)
        higher = jnp.maximum(running_top, jnp.max(scores, axis=2))
        total_sum = total_sum * jnp.exp(running_top - higher) + jnp.sum(
            jnp.exp(scores - higher[:, :, None]), axis=2
        )
        return ((higher, total_sum), None)

    start_state = (
        jnp.full((head_count, row_count), -1e30, jnp.float32),
        jnp.zeros((head_count, row_count), jnp.float32),
    )
    (running_top, total_sum), unused = lax.scan(
        running_total, start_state, (key_blocks, block_starts)
    )
    log_total = running_top + jnp.log(total_sum)

    def attend_block(attend_acc, block_items):
        key_part, value_part, block_start = block_items
        prob_bf = jnp.exp(block_scores(key_part, block_start) - log_total[:, :, None]).astype(
            jnp.bfloat16
        )
        return (
            attend_acc
            + jnp.einsum("htk,khd->thd", prob_bf, value_part, preferred_element_type=jnp.float32),
            None,
        )

    attend_acc, unused = lax.scan(
        attend_block,
        jnp.zeros((row_count, head_count, HEAD_DIM), jnp.float32),
        (key_blocks, value_blocks, block_starts),
    )
    attended = attend_acc.reshape(row_count, channels).astype(jnp.bfloat16)
    frame_live = (first_row + jnp.arange(row_count, dtype=jnp.int32) < length)[:, None]
    hidden = (frames.astype(jnp.float32) + attended.astype(jnp.float32)).astype(jnp.bfloat16)
    masked = jnp.where(frame_live, hidden, jnp.zeros_like(hidden))
    past_rows = shifted(masked[row_count - (KERNEL - 1) :], "seq", 1)
    extended = jnp.concatenate([past_rows, masked], axis=0).astype(jnp.float32)
    weights = conv_kernel.astype(jnp.float32)
    conv_out = jnp.zeros((row_count, channels), jnp.float32)
    for tap_index in range(KERNEL):
        conv_out = (
            conv_out
            + weights[tap_index]
            * extended[KERNEL - 1 - tap_index : KERNEL - 1 - tap_index + row_count]
        )
    sig_conv = jax.nn.sigmoid(conv_out)
    out = (hidden.astype(jnp.float32) + conv_out * sig_conv).astype(jnp.bfloat16)
    loss_grad = jnp.where(frame_live, upstream.astype(jnp.float32), 0.0)
    conv_grad = (loss_grad * sig_conv * (1.0 + conv_out * (1.0 - sig_conv))).astype(jnp.bfloat16)
    conv_float = conv_grad.astype(jnp.float32)
    kernel_part = jnp.stack(
        [
            jnp.sum(
                conv_float * extended[KERNEL - 1 - tap_index : KERNEL - 1 - tap_index + row_count],
                axis=0,
            )
            for tap_index in range(KERNEL)
        ]
    )
    future_rows = shifted(conv_grad[: KERNEL - 1], "seq", -1)
    ahead_rows = jnp.concatenate([conv_grad, future_rows], axis=0).astype(jnp.float32)
    back_conv = jnp.zeros((row_count, channels), jnp.float32)
    for tap_index in range(KERNEL):
        back_conv = back_conv + weights[tap_index] * ahead_rows[tap_index : tap_index + row_count]
    frame_grad = (loss_grad + jnp.where(frame_live, back_conv, 0.0)).astype(jnp.bfloat16)
    grad_heads = frame_grad.reshape(row_count, head_count, HEAD_DIM)
    attended_heads = attended.reshape(row_count, head_count, HEAD_DIM)
    delta_rows = jnp.sum(
        grad_heads.astype(jnp.float32) * attended_heads.astype(jnp.float32), axis=2
    ).T

    def score_grads(key_part, value_part, block_start):
        soft_weights = jnp.exp(block_scores(key_part, block_start) - log_total[:, :, None])
        prob_grad = jnp.einsum(
            "thd,khd->htk", grad_heads, value_part, preferred_element_type=jnp.float32
        )
        score_grad = (soft_weights * (prob_grad - delta_rows[:, :, None])).astype(jnp.bfloat16)
        return (soft_weights.astype(jnp.bfloat16), score_grad)

    def gradient_block(query_acc, block_items):
        key_part, value_part, block_start = block_items
        prob_bf, score_grad = score_grads(key_part, value_part, block_start)
        query_acc = query_acc + jnp.einsum(
            "htk,khd->thd", score_grad, key_part, preferred_element_type=jnp.float32
        )
        key_term = (
            jnp.einsum("htk,thd->khd", score_grad, query_heads, preferred_element_type=jnp.float32)
            * score_scale
        )
        value_term = jnp.einsum(
            "htk,thd->khd", prob_bf, grad_heads, preferred_element_type=jnp.float32
        )
        grad_terms = jnp.concatenate(
            [key_term.reshape(key_block, channels), value_term.reshape(key_block, channels)], axis=1
        )
        return (query_acc, grad_terms)

    query_acc, grad_terms = lax.scan(
        gradient_block,
        jnp.zeros((row_count, head_count, HEAD_DIM), jnp.float32),
        (key_blocks, value_blocks, block_starts),
    )
    own_rows = lax.psum_scatter(
        grad_terms.reshape(span, 2 * channels).astype(jnp.bfloat16),
        "seq",
        scatter_dimension=0,
        tiled=True,
    ).astype(jnp.float32)
    key_grad = own_rows[:, :channels].astype(jnp.bfloat16)
    value_grad = own_rows[:, channels:].astype(jnp.bfloat16)
    query_grad = (query_acc * score_scale).reshape(row_count, channels).astype(jnp.bfloat16)
    kernel_total = lax.psum(kernel_part, ("dp", "seq"))
    kernel_grad = kernel_total / lax.axis_size("dp")
    return (out, query_grad, key_grad, value_grad, frame_grad, kernel_grad)


def solution(mesh):
    placed = (
        P(("dp", "seq"), None),
        P(("dp", "seq"), None),
        P(("dp", "seq"), None),
        P(("dp", "seq"), None),
        P(("dp", "seq"), None),
        P("dp"),
        P(),
    )
    return jax.shard_map(
        per_device,
        mesh=mesh,
        in_specs=placed,
        out_specs=(
            P(("dp", "seq"), None),
            P(("dp", "seq"), None),
            P(("dp", "seq"), None),
            P(("dp", "seq"), None),
            P(("dp", "seq"), None),
            P(),
        ),
        check_vma=False,
    )
```

profile of v0, /device:TPU:1, one launch (start us, length us, event | category | flops | bytes accessed | tf_op | source)
XLA Modules:
  0.0 772.7 jit_solution(14482289051030039429)
XLA Ops:
  13.8 92.2 %all-gather.5.cloned.1.call-done = bf16[2560,768]{1,0:T(8,128)(2,1)} async-done(((bf16[160,768]{1,0:T(8,128)(2,1)}), bf16[2560,768]{1,0:T(8,128)(2,1)}) %all-gather.5.cloned.1.call-update) | async-done | bytes 3932176 | tf_op jit(solution)/shard_map/all_gather | solution.py:31
  106.1 6.2 copy.23
  112.3 7.6 reshape.64
  119.9 82.5 %all-gather.3.cloned.1.call-done = bf16[2560,768]{1,0:T(8,128)(2,1)} async-done(((bf16[160,768]{1,0:T(8,128)(2,1)}), bf16[2560,768]{1,0:T(8,128)(2,1)}) %all-gather.3.cloned.1.call-update) | async-done | bytes 3932176 | tf_op jit(solution)/shard_map/all_gather | solution.py:32
  202.4 6.2 copy.22
  208.6 7.6 reshape.63
  216.2 5.0 copy.26
  221.2 2.7 copy.25
  223.9 22.7 %while.37 = (s32[]{:T(128)}, f32[12,160]{1,0:T(8,128)S(1)}, f32[12,160]{1,0:T(8,128)S(1)}, s32[4]{0:T(128)S(1)}, s32[]{:T(128)}, /*index=5*/bf16[4,640,12,64]{1,...) while((s32[]{:T(128)}, f32[12,160]{1,0:T(8,128)S(1)}, ...), condition=%wide.region_3.4_spmd.clone, body=%wide.region_0.3_spmd.clone.sunk | while | flops 165898880 | bytes 11161096 | solution.py:61
  225.8 2.2 bitcast_reduce_fusion.2
  228.0 1.5 fusion.145
  231.5 2.2 bitcast_reduce_fusion.2
  233.7 1.5 fusion.145
  237.2 2.2 bitcast_reduce_fusion.2
  239.4 1.5 fusion.145
  242.8 2.2 bitcast_reduce_fusion.2
  246.6 43.0 %while.38 = (s32[]{:T(128)}, f32[160,12,64]{0,2,1:T(8,128)}, bf16[4,640,12,64]{1,3,2,0:T(8,128)(2,1)}, s32[4]{0:T(128)S(1)}, s32[]{:T(128)}, /*index=5*/bf16[4,6...) while((s32[]{:T(128)}, f32[160,12,64]{0,2,1:T(8,128)}, ...), condition=%wide.region_5.6_spmd.clone, body=%wide.region_4.5_spmd.clone.sunk | while | flops 319735040 | bytes 5464979 | solution.py:77
  248.5 4.5 constant_dynamic-slice_fusion.2
  253.0 4.2 fusion.150
  259.1 4.5 constant_dynamic-slice_fusion.2
  263.6 4.4 fusion.150
  269.9 4.5 constant_dynamic-slice_fusion.2
  274.4 4.4 fusion.150
  280.7 4.5 constant_dynamic-slice_fusion.2
  285.2 4.4 fusion.150
  291.1 2.7 collective-permute-start
  293.8 1.9 slice_reduce_fusion.30
  297.1 14.6 %fusion.79 = (f32[768]{0:T(1024)S(1)}, f32[768]{0:T(1024)S(1)}, f32[768]{0:T(1024)S(1)}, f32[768]{0:T(1024)S(1)}, f32[768]{0:T(1024)S(1)}, /*index=5*/f32[768]{0...) fusion(f32[191,768]{0,1:T(8,128)S(1)} %maximum_convert_fusion, ...), kind=kLoop, calls=%fused_computation.121 | loop fusion | flops 13625856 | bytes 16865440 | tf_op jit(solution)/shard_map/reduce_sum | solution.py:103
  312.9 4.7 fusion.78
  336.5 5.4 stack.131
  342.4 13.5 %fusion.83 = bf16[160,768]{0,1:T(8,128)(2,1)S(1)} fusion(f32[191,768]{0,1:T(8,128)S(1)} %maximum_convert_fusion.1, bf16[160,768]{0,1:T(8,128)(2,1)S(1)} %copy.29, f32[768]{0:T(1024)S(1)} %get-tuple-element.320, f32[768]{0:T(1024)S(1)} %get-tuple-element.321, f32[768]{0:T(1024)S(1)} %get-tuple-element.322, f32[768]{0:T(1024)} %get-tuple-element.323, ...), kind=kLoop, calls=%fused_computation.126 | loop fusion | flops 8355840 | bytes 16318624 | tf_op jit(solution)/shard_map/convert_element_type | solution.py:115
  356.1 50.8 %while.39 = (s32[]{:T(128)}, f32[160,12,64]{0,2,1:T(8,128)S(1)}, bf16[4,640,1536]{1,2,0:T(8,128)(2,1)}, bf16[4,640,12,64]{1,3,2,0:T(8,128)(2,1)}, s32[4]{0:T(128...) while((s32[]{:T(128)}, f32[160,12,64]{0,2,1:T(8,128)S(1)}, ...), condition=%wide.region_8.9_spmd.clone, body=%wide.region_7.8_spmd.clone.sunk | while | flops 803882240 | bytes 32956980 | solution.py:148
  358.0 2.1 fusion.161
  361.4 3.0 multiply_convert_fusion.5
  364.4 2.4 fusion.162
  370.7 2.1 fusion.161
  374.1 3.0 multiply_convert_fusion.5
  377.1 2.4 fusion.162
  383.4 2.1 fusion.161
  386.8 3.0 multiply_convert_fusion.5
  389.8 2.4 fusion.162
  396.1 2.1 fusion.161
  399.5 3.0 multiply_convert_fusion.5
  402.5 2.4 fusion.162
  406.9 10.7 %copy.32 = bf16[4,640,1536]{2,1,0:T(8,128)(2,1)} copy(bf16[4,640,1536]{1,2,0:T(8,128)(2,1)} %get-tuple-element.148) | data formatting | bytes 15728640 | tf_op jit(solution)/shard_map/convert_element_type | solution.py:154
  421.6 172.5 %all-reduce.2.cloned.1.call-done = f32[32,768]{1,0:T(8,128)} async-done(((f32[32,768]{1,0:T(8,128)}), f32[32,768]{1,0:T(8,128)}) %all-reduce.2.cloned.1.call-update) | async-done | bytes 98320 | tf_op jit(solution)/shard_map/psum | solution.py:162
  595.6 168.7 %reduce-scatter.2.cloned.1.call-done = bf16[160,1536]{1,0:T(8,128)(2,1)} async-done(((bf16[2560,1536]{1,0:T(8,128)(2,1)}), bf16[160,1536]{1,0:T(8,128)(2,1)}) %reduce-scatter.2.cloned.1.call-update) | async-done | bytes 491536 | tf_op jit(solution)/shard_map/reduce_scatter | solution.py:153
  764.3 1.9 fusion.115
  (137 shorter events, 72.6 us)
Async XLA Ops:
  7.2 98.9 %all-gather.5.cloned.1.call-start = ((), (), s32[]{:S(2)}) async-start(), calls=%async_computation.2 | async-start | bytes 4177920 | tf_op jit(solution)/shard_map/all_gather | solution.py:31
  7.9 194.5 %all-gather.3.cloned.1.call-start = ((), (), s32[]{:S(2)}) async-start(), calls=%async_computation.1 | async-start | bytes 4177920 | tf_op jit(solution)/shard_map/all_gather | solution.py:32
  8.6 585.4 %all-reduce.2.cloned.1.call-start = ((), (), s32[]{:S(2)}) async-start(), calls=%async_computation.4 | async-start | bytes 196608 | tf_op jit(solution)/shard_map/psum | solution.py:162
  10.2 102.1 %copy-start.3 = (f32[32,768]{1,0:T(8,128)}, f32[32,768]{1,0:T(8,128)S(1)}, u32[]{:S(2)}) copy-start(f32[32,768]{1,0:T(8,128)S(1)} %convert_element_type.78) | copy-start | bytes 294916
  13.1 277.8 %copy-start.6 = (pred[160]{0:T(512)(128)(4,1)}, pred[160]{0:T(512)(128)(4,1)S(1)}, u32[]{:S(2)}) copy-start(pred[160]{0:T(512)(128)(4,1)S(1)} %add_compare_fusion.3) | copy-start | bytes 484
  216.2 5.0 copy-start
  289.6 6.1 copy-start.4
  289.6 6.1 copy-start.7
  291.1 5.8 collective-permute-start
  311.6 30.6 %collective-permute-start.1 = (bf16[31,768]{0,1:T(8,128)(2,1)S(1)}, bf16[31,768]{0,1:T(8,128)(2,1)S(1)}, u32[]{:S(2)}, u32[]{:S(2)}) collective-permute-start(bf16[31,768]{0,1:T(8,128)(2,1)S(1)} %slice.531), channel_id=1, source_target_pairs={{1,0},{2,1},{3,2},{4,3},{5,4},{6,5},{7,6},{8,7},{9,8},{10,9},{11,1... | collective-permute-start | bytes 142856 | tf_op jit(solution)/shard_map/ppermute | solution.py:13
  342.0 422.3 %reduce-scatter.2.cloned.1.call-start = ((), (), s32[]{:S(2)}) async-start(), calls=%async_computation.3 | async-start | bytes 8355840 | tf_op jit(solution)/shard_map/reduce_scatter | solution.py:153
  342.4 13.5 %copy-start.2 = (f32[160,12,64]{0,2,1:T(8,128)S(1)}, f32[160,12,64]{0,2,1:T(8,128)}, u32[]{:S(2)}) copy-start(f32[160,12,64]{0,2,1:T(8,128)} %get-tuple-element.146) | copy-start | bytes 1474564
  342.4 13.7 %copy-start.5 = (f32[12,160]{1,0:T(8,128)S(1)}, f32[12,160]{1,0:T(8,128)}, u32[]{:S(2)}) copy-start(f32[12,160]{1,0:T(8,128)} %copy-done.4) | copy-start | bytes 23044
  342.4 13.7 %copy-start.8 = (s32[4]{0:T(128)S(1)}, s32[4]{0:T(128)}, u32[]{:S(2)}) copy-start(s32[4]{0:T(128)} %copy-done.7) | copy-start | bytes 52
  417.6 1.1 copy-start.1
Sparse Core Ops, SparseCore 0:
  9.8 96.2 all-gather.4
  107.8 94.5 all-gather.2
  342.1 251.9 all-reduce.1
  596.5 167.7 reduce-scatter.1
where the time goes:
time: 775 us; the launch traced here: 773 us
  waiting for transfers between devices  517 us (67%)
  local copies, waits for them, and re-layouts  108 us (14%)
  other arithmetic  64.8 us (8%)
  matrix products  63.5 us (8%)
  between operations  14.7 us (2%)
    psum x1, waiting for transfers between devices, per_device(): kernel_total = lax.psum(kernel_part, ('dp', 'seq'))  173 us
    reduce_scatter x1, waiting for transfers between devices, per_device(): lax.psum_scatter(grad_terms.reshape(span, 2 * channels).astype(jnp.bfloat...  169 us
    all_gather x1, waiting for transfers between devices, per_device(): lax.all_gather(keys, 'seq', axis=0, tiled=True)  92.2 us
    all_gather x1, waiting for transfers between devices, per_device(): lax.all_gather(values, 'seq', axis=0, tiled=True)  82.5 us
    dynamic_slice x16, local copies, waits for them, and re-layouts, per_device(): lax.scan(running_total, start_state, (key_blocks, block_starts))  24.9 us
    another operation x33, local copies, waits for them, and re-layouts, per_device(): jnp.stack([jnp.sum(conv_float * extended[KERNEL - 1 - tap_index:KERNEL -...  24.3 us
    reduce_sum x2, other arithmetic, per_device(): jnp.sum(conv_float * extended[KERNEL - 1 - tap_index:KERNEL - 1 - tap_ind...  19.2 us
    dot_general x4, matrix products, attend_block(): jnp.einsum('htk,khd->thd', prob_bf, value_part, preferred_element_type=jn...  17.5 us
  transfers between devices with their start and end apart: 6, of which 4 were waited for; matrix products, arithmetic and copies ran while one was open for 17% of the time, Pallas kernels for 0%

commit v1 on v0

--- a/solution.py
+++ b/solution.py
@@ -159,7 +159,8 @@
     key_grad = own_rows[:, :channels].astype(jnp.bfloat16)
     value_grad = own_rows[:, channels:].astype(jnp.bfloat16)
     query_grad = (query_acc * score_scale).reshape(row_count, channels).astype(jnp.bfloat16)
-    kernel_total = lax.psum(kernel_part, ("dp", "seq"))
+    main = lax.all_gather(kernel_part, ("dp", "seq"))
+    kernel_total = jnp.sum(main, axis=0)
     kernel_grad = kernel_total / lax.axis_size("dp")
     return (out, query_grad, key_grad, value_grad, frame_grad, kernel_grad)
 

time: 775 us -> 1350 us (1.74)
  waiting for transfers between devices: 517 us -> 1090 us
  local copies, waits for them, and re-layouts: 108 us -> 68.3 us
  matrix products: 63.5 us -> 83.4 us
    all_gather x0 -> x1, waiting for transfers between devices: none -> 744 us  [per_device(): main = lax.all_gather(kernel_part, ('dp', 'seq'))]
    psum x1 -> x0, waiting for transfers between devices: 173 us -> none  [per_device(): kernel_total = lax.psum(kernel_part, ('dp', 'seq'))]
    another operation x33, local copies, waits for them, and re-layouts: 24.3 us -> 2.73 us  [per_device(): jnp.stack([jnp.sum(conv_float * extended[KERNEL - 1 - tap_index:KERNEL -...]
    dynamic_slice x16 -> x12, local copies, waits for them, and re-layouts: 24.9 us -> 7.37 us  [per_device(): lax.scan(running_total, start_state, (key_blocks, block_starts))]
    all_gather x1, waiting for transfers between devices: 92.2 us -> 77.7 us  [per_device(): lax.all_gather(keys, 'seq', axis=0, tiled=True)]
  transfers between devices with their start and end apart: 6 -> 6, of which waited for: 4 -> 6; matrix products, arithmetic and copies ran while one was open for 17% -> 3% of each run, Pallas kernels for 0% -> 0%
where the time goes in v1:
time: 1350 us; the launch traced here: 1340 us
  waiting for transfers between devices  1090 us (81%)
  matrix products  83.4 us (6%)
  other arithmetic  77.9 us (6%)
  local copies, waits for them, and re-layouts  68.3 us (5%)
  between operations  15.1 us (1%)
    all_gather x1, waiting for transfers between devices, per_device(): main = lax.all_gather(kernel_part, ('dp', 'seq'))  744 us
    reduce_scatter x1, waiting for transfers between devices, per_device(): lax.psum_scatter(grad_terms.reshape(span, 2 * channels).astype(jnp.bfloat...  166 us
    all_gather x1, waiting for transfers between devices, per_device(): lax.all_gather(values, 'seq', axis=0, tiled=True)  92.6 us
    all_gather x1, waiting for transfers between devices, per_device(): lax.all_gather(keys, 'seq', axis=0, tiled=True)  77.7 us
  transfers between devices with their start and end apart: 6, of which 6 were waited for; matrix products, arithmetic and copies ran while one was open for 3% of the time, Pallas kernels for 0%

profile of v1, /device:TPU:1, one launch (start us, length us, event | category | flops | bytes accessed | tf_op | source)
XLA Modules:
  0.0 1339.5 jit_solution(7572825218616453015)
XLA Ops:
  13.4 92.6 %all-gather.5.cloned.1.call-done = bf16[2560,768]{1,0:T(8,128)(2,1)} async-done(((bf16[160,768]{1,0:T(8,128)(2,1)}), bf16[2560,768]{1,0:T(8,128)(2,1)}) %all-gather.5.cloned.1.call-update) | async-done | bytes 3932176 | tf_op jit(solution)/shard_map/all_gather | solution.py:32
  106.1 6.2 copy.37
  112.3 7.6 reshape.63
  119.9 4.8 copy.41
  124.7 77.7 %all-gather.7.cloned.1.call-done = bf16[2560,768]{1,0:T(8,128)(2,1)} async-done(((bf16[160,768]{1,0:T(8,128)(2,1)}), bf16[2560,768]{1,0:T(8,128)(2,1)}) %all-gather.7.cloned.1.call-update) | async-done | bytes 3932176 | tf_op jit(solution)/shard_map/all_gather | solution.py:31
  202.4 6.2 copy.38
  208.7 7.6 reshape.64
  216.3 4.7 copy.42
  221.0 39.7 %while.37 = (s32[]{:T(128)}, f32[12,160]{1,0:T(8,128)S(1)}, f32[12,160]{1,0:T(8,128)S(1)}, s32[4]{0:T(128)S(1)}, s32[]{:T(128)}, /*index=5*/bf16[4,640,12,64]{1,...) while((s32[]{:T(128)}, f32[12,160]{1,0:T(8,128)S(1)}, f32[12,160]{1,0:T(8,128)S(1)}, ...), condition=%wide.region_3.4_spmd.clone, body=%wide.region_0.3_spmd.clone.sunk | while | flops 165898880 | bytes 11308552 | solution.py:61
  222.9 4.4 bitcast_reduce_fusion.2
  227.3 3.6 fusion.145
  232.8 4.3 bitcast_reduce_fusion.2
  237.2 3.6 fusion.145
  242.8 4.4 bitcast_reduce_fusion.2
  247.1 3.6 fusion.145
  252.7 4.4 bitcast_reduce_fusion.2
  257.1 3.6 fusion.145
  260.8 23.3 %while.38 = (s32[]{:T(128)}, f32[160,12,64]{0,2,1:T(8,128)S(1)}, bf16[4,640,12,64]{1,3,2,0:T(8,128)(2,1)}, s32[4]{0:T(128)S(1)}, s32[]{:T(128)}, /*index=5*/bf16...) while((s32[]{:T(128)}, f32[160,12,64]{0,2,1:T(8,128)S(1)}, ...), condition=%wide.region_5.6_spmd.clone, body=%wide.region_4.5_spmd.clone.sunk | while | flops 319735040 | bytes 3352970 | solution.py:77
  262.7 3.9 fusion.150
  268.5 3.9 fusion.150
  274.3 3.9 fusion.150
  280.2 3.9 fusion.150
  285.3 2.6 collective-permute-start
  288.2 2.3 collective-permute-done
  290.7 13.6 %fusion.78 = (f32[768]{0:T(1024)S(1)}, f32[768]{0:T(1024)}, f32[768]{0:T(1024)}, f32[768]{0:T(1024)}, f32[768]{0:T(1024)}, /*index=5*/f32[768]{0:T(1024)}, f32[7...) fusion(f32[191,768]{0,1:T(8,128)S(1)} %maximum_convert_fusion, ...), kind=kLoop, calls=%fused_computation.119 | loop fusion | flops 13625856 | bytes 16865440 | tf_op jit(solution)/shard_map/reduce_sum | solution.py:103
  305.8 6.3 collective-permute-done.1
  312.2 10.8 fusion.82
  323.8 64.2 %while.39 = (s32[]{:T(128)}, f32[160,12,64]{0,2,1:T(8,128)}, bf16[4,640,1536]{1,2,0:T(8,128)(2,1)}, bf16[4,640,12,64]{1,3,2,0:T(8,128)(2,1)}, s32[4]{0:T(128)S(1...) while((s32[]{:T(128)}, f32[160,12,64]{0,2,1:T(8,128)}, ...), condition=%wide.region_8.9_spmd.clone, body=%wide.region_7.8_spmd.clone.sunk | while | flops 803882240 | bytes 73704064 | solution.py:148
  327.9 3.0 multiply_convert_fusion.5
  330.9 3.3 fusion.162
  334.2 2.3 fusion.163
  339.6 2.2 fusion.161
  343.8 3.0 multiply_convert_fusion.5
  346.8 3.6 fusion.162
  350.3 2.3 fusion.163
  359.9 3.0 multiply_convert_fusion.5
  362.9 3.6 fusion.162
  366.4 2.3 fusion.163
  371.8 2.2 fusion.161
  376.0 3.0 multiply_convert_fusion.5
  379.0 3.6 fusion.162
  382.5 2.3 fusion.163
  387.9 10.7 copy.46
  399.7 4.7 fusion.77
  404.9 2.6 stack.131
  411.6 165.7 %reduce-scatter.2.cloned.1.call-done = bf16[160,1536]{1,0:T(8,128)(2,1)} async-done(((bf16[2560,1536]{1,0:T(8,128)(2,1)}), bf16[160,1536]{1,0:T(8,128)(2,1)}) %reduce-scatter.2.cloned.1.call-update) | async-done | bytes 491536 | tf_op jit(solution)/shard_map/reduce_scatter | solution.py:153
  579.1 743.8 %all-gather.9.cloned.1.call-done = f32[8192,768]{1,0:T(8,128)} async-done(((f32[32,768]{1,0:T(8,128)}), f32[8192,768]{1,0:T(8,128)}) %all-gather.9.cloned.1.call-update) | async-done | bytes 25165840 | tf_op jit(solution)/shard_map/all_gather | solution.py:162
  1322.9 9.4 reduce_sum.348
  (187 shorter events, 56.5 us)
Async XLA Ops:
  7.2 98.9 %all-gather.5.cloned.1.call-start = ((), (), s32[]{:S(2)}) async-start(), calls=%async_computation.1 | async-start | bytes 4177920 | tf_op jit(solution)/shard_map/all_gather | solution.py:32
  7.9 194.5 %all-gather.7.cloned.1.call-start = ((), (), s32[]{:S(2)}) async-start(), calls=%async_computation.2 | async-start | bytes 4177920 | tf_op jit(solution)/shard_map/all_gather | solution.py:31
  8.6 568.6 %reduce-scatter.2.cloned.1.call-start = ((), (), s32[]{:S(2)}) async-start(), calls=%async_computation.3 | async-start | bytes 8355840 | tf_op jit(solution)/shard_map/reduce_scatter | solution.py:153
  12.4 271.8 %copy-start.7 = (bf16[160,768]{0,1:T(8,128)(2,1)}, bf16[160,768]{0,1:T(8,128)(2,1)S(1)}, u32[]{:S(2)}) copy-start(bf16[160,768]{0,1:T(8,128)(2,1)S(1)} %copy.36) | copy-start | bytes 737284
  260.8 27.3 %copy-start.12 = (bf16[160,768]{1,0:T(8,128)(2,1)S(1)}, bf16[160,768]{1,0:T(8,128)(2,1)}, u32[]{:S(2)}) copy-start(bf16[160,768]{1,0:T(8,128)(2,1)} %param.17) | copy-start | bytes 737284
  284.2 0.9 copy-start.3
  285.3 5.2 collective-permute-start
  304.2 18.8 %copy-start.5 = (bf16[160,768]{0,1:T(8,128)(2,1)}, bf16[160,768]{0,1:T(8,128)(2,1)S(1)}, u32[]{:S(2)}) copy-start(bf16[160,768]{0,1:T(8,128)(2,1)S(1)} %get-tuple-element.435) | copy-start | bytes 737284
  304.3 7.8 collective-permute-start.1
  323.0 0.7 copy-start.9
  323.8 4.1 copy-start.10
  325.9 4.9 copy-start
  330.9 3.3 copy-start.1
  339.6 4.1 copy-start.10
  341.8 4.9 copy-start
  346.8 3.6 copy-start.1
  355.7 4.1 copy-start.10
  357.9 4.9 copy-start
  362.9 3.6 copy-start.1
  371.8 4.1 copy-start.10
  374.0 4.9 copy-start
  379.0 3.6 copy-start.1
  398.6 1.0 copy-start.6
  398.6 8.9 copy-start.4
  398.6 8.9 copy-start.8
  398.7 11.1 copy-start.11
  398.7 12.0 copy-start.2
  398.7 924.2 %all-gather.9.cloned.1.call-start = ((), (), s32[]{:S(2)}) async-start(), calls=%async_computation.4 | async-start | bytes 25264128 | tf_op jit(solution)/shard_map/all_gather | solution.py:162
  399.6 4.8 copy-start.26
  399.6 4.9 copy-start.25
  399.6 4.9 copy-start.24
  399.6 4.9 copy-start.23
  399.6 4.9 copy-start.22
  399.6 4.9 copy-start.21
  399.6 4.9 copy-start.20
  399.6 4.9 copy-start.19
  399.7 5.0 copy-start.18
  399.7 5.0 copy-start.17
  399.7 5.0 copy-start.16
  399.7 5.0 copy-start.15
  399.7 5.0 copy-start.14
  399.7 5.0 copy-start.13
Sparse Core Ops, SparseCore 0:
  9.8 96.2 all-gather.4
  107.8 94.5 all-gather.6
  398.8 178.4 reduce-scatter.1
  579.5 743.2 all-gather.8
